TPU v7x, 256 devices: a whole 4x4x8 slice. The times are simulated.
256 devices in a mesh: dp: 8 (over x, z_lo), seq: 32 (over z_hi, y, core).
Axes of the slice: x: 4, y: 4, z: 8 (z_hi: 4, z_lo: 2; z = z_hi * 2 + z_lo), core: 2. Of those that a mesh axis runs over, the one named last changes fastest.
Arguments:
- inputs: float32 [8, 4096, 2048], P('dp', 'seq'), may hold values from -6 to 6
- cotangent: float32 [8, 4096, 2048], P('dp', 'seq'), may hold values from -6 to 6
- block_mix: float32 [128, 128], replicated, may hold values from -0.5 to 0.5
- twist_hi: float32 [2, 2, 2048], replicated, may hold values from -3 to 3
- twist_lo: float32 [2, 2, 2048], replicated, may hold values from -3 to 3
- gain: float32 [2048], replicated, may hold values from 0.5 to 1.5
- gate_up: float32 [128, 2, 16, 256], P('seq'), may hold values from -0.5 to 0.5
- down: float32 [256, 16, 128], P('seq'), may hold values from -0.375 to 0.375
Outputs:
- grad_inputs: float32 [8, 4096, 2048], P('dp', 'seq')
- grad_gate_up: float32 [128, 2, 16, 256], P('seq')
- grad_down: float32 [256, 16, 128], P('seq')
- grad_block_mix: float32 [128, 128], replicated
- grad_twist_hi: float32 [2, 2, 2048], replicated
- grad_twist_lo: float32 [2, 2, 2048], replicated
- grad_gain: float32 [2048], replicated
All inputs are finite; a program needn't handle non-finite values.
Results may differ from a plain program's by a relative error of at most 0.00022.
Values sent between devices are 32-bit elements; how exact they have to be, the bound alone decides.
No kernel may reach another device: no remote copies, remote signals or barrier semaphores. Data moves between devices by JAX's collectives and lax.ppermute only.
A program may use at most 64 MiB of HBM per device.

v0:
```python
import math
import jax
import jax.numpy as jnp
from jax import lax
from jax.sharding import PartitionSpec as P

NB = 16
BLK = 128
DB = 128
HIGH = lax.Precision.HIGHEST
EPS = 1e-05


def from_partner(block, axis, distance):
    count = lax.axis_size(axis)
    route = []
    for low in range(count):
        high = low | 1 << distance
        if high != low and high < count:
            route += [(low, high), (high, low)]
    return lax.ppermute(block, axis, route)


def side_of(bit):
    return lax.axis_index("seq") // (1 << bit) % 2


def forward_section(field, coeff, bit):
    partner = from_partner(field, "seq", bit)
    own = coeff[side_of(bit)]
    return (own[0] * field + own[1] * partner, partner)


def backward_section(grad, field, partner, coeff, bit):
    side = side_of(bit)
    own = coeff[side]
    sent = from_partner(own[1] * grad, "seq", bit)
    back = own[0] * grad + sent
    term = jnp.stack([jnp.sum(grad * field, axis=0), jnp.sum(grad * partner, axis=0)])
    pick = (jnp.arange(2) == side).astype(jnp.float32)
    return (back, pick[:, None, None] * term[None])


def exchange(x):
    return lax.all_to_all(x, "seq", 0, 0, tiled=True)


def to_blocks(field, count):
    tokens = field.shape[0]
    halves = count // NB
    x = field.reshape(halves, tokens // halves, NB, DB)
    x = jnp.transpose(x, (2, 0, 1, 3))
    return x.reshape(count, tokens // halves, DB)


def from_blocks(x, tokens, count):
    halves = count // NB
    x = x.reshape(NB, halves, tokens // halves, DB)
    x = jnp.transpose(x, (1, 2, 0, 3))
    return x.reshape(tokens, NB * DB)


def per_device(inputs, cotangent, block_mix, twist_hi, twist_lo, gain, gate_up, down):
    seq_in = inputs[0]
    tokens, width = seq_in.shape
    count = lax.axis_size("seq")
    halves = count // NB
    top_bit = count.bit_length() - 2
    nblocks = tokens // BLK
    rows_gu = gate_up.shape[0]
    rows_dn = down.shape[0]
    fb = gate_up.shape[3]
    gu_n = jnp.transpose(gate_up, (2, 0, 1, 3)).reshape(NB, rows_gu * 2 * fb)
    dn_n = jnp.transpose(down, (1, 0, 2)).reshape(NB, rows_dn * DB)
    wbuf = jnp.concatenate([gu_n, dn_n], axis=1)
    wbuf = jnp.repeat(wbuf, halves, axis=0)
    wrecv = exchange(wbuf)
    w_gu = wrecv[:, : rows_gu * 2 * fb].reshape(count * rows_gu, 2, fb)
    w_dn = wrecv[:, rows_gu * 2 * fb :].reshape(count * rows_dn, DB)
    grad_out = cotangent[0]
    cot_blk = exchange(to_blocks(grad_out, count)).reshape(-1, DB)
    xb = seq_in.reshape(nblocks, BLK, width)
    mixed = jnp.einsum("ij,kjd->kid", block_mix, xb, precision=HIGH).reshape(tokens, width)
    first, mixed_peer = forward_section(mixed, twist_hi, top_bit)
    second, first_peer = forward_section(first, twist_lo, 0)
    resid = seq_in + second
    scale = lax.rsqrt(jnp.mean(resid * resid, axis=-1, keepdims=True) + EPS)
    unit = resid * scale
    normed = unit * gain
    x_blk = exchange(to_blocks(normed, count)).reshape(-1, DB)
    gate_val = jnp.dot(x_blk, w_gu[:, 0], precision=HIGH)
    up_val = jnp.dot(x_blk, w_gu[:, 1], precision=HIGH)
    sig = jax.nn.sigmoid(gate_val)
    act = gate_val * sig
    hidden = act * up_val
    grad_hidden = jnp.dot(cot_blk, w_dn.T, precision=HIGH)
    grad_gate = grad_hidden * up_val * sig * (1.0 + gate_val * (1.0 - sig))
    grad_up = grad_hidden * act
    grad_x = jnp.dot(grad_gate, w_gu[:, 0].T, precision=HIGH) + jnp.dot(
        grad_up, w_gu[:, 1].T, precision=HIGH
    )
    grad_normed = from_blocks(exchange(grad_x.reshape(count, -1, DB)), tokens, count)
    d_gate = jnp.dot(x_blk.T, grad_gate, precision=HIGH)
    d_up = jnp.dot(x_blk.T, grad_up, precision=HIGH)
    d_gu = jnp.stack([d_gate, d_up], axis=1).reshape(count, rows_gu * 2 * fb)
    d_dn = jnp.dot(hidden.T, cot_blk, precision=HIGH).reshape(count, rows_dn * DB)
    grecv = exchange(jnp.concatenate([d_gu, d_dn], axis=1))
    grecv = grecv.reshape(NB, halves, -1).sum(axis=1)
    part_gu = jnp.transpose(grecv[:, : rows_gu * 2 * fb].reshape(NB, rows_gu, 2, fb), (1, 2, 0, 3))
    part_down = jnp.transpose(grecv[:, rows_gu * 2 * fb :].reshape(NB, rows_dn, DB), (1, 0, 2))
    part_gu, part_down = lax.psum((part_gu, part_down), "dp")
    grad_gain_local = jnp.sum(grad_normed * unit, axis=0)
    weighted = grad_normed * gain
    inner = jnp.mean(weighted * resid, axis=-1, keepdims=True)
    grad_resid = grad_out + scale * weighted - resid * scale * scale * scale * inner
    grad_first, term_lo = backward_section(grad_resid, first, first_peer, twist_lo, 0)
    grad_mixed, term_hi = backward_section(grad_first, mixed, mixed_peer, twist_hi, top_bit)
    grad_mb = grad_mixed.reshape(nblocks, BLK, width)
    term_block = jnp.einsum("kid,kjd->ij", grad_mb, xb, precision=HIGH)
    grad_seq = jnp.einsum("ij,kid->kjd", block_mix, grad_mb, precision=HIGH).reshape(tokens, width)
    grad_seq = grad_seq + grad_resid
    sum_block, sum_hi, sum_lo, sum_gain = lax.psum(
        (term_block, term_hi, term_lo, grad_gain_local), ("dp", "seq")
    )
    factor = 1.0 / math.sqrt(lax.axis_size("dp") * count * tokens)
    return (
        grad_seq[None],
        part_gu * factor,
        part_down * factor,
        sum_block * factor,
        sum_hi * factor,
        sum_lo * factor,
        sum_gain * factor,
    )


def solution(mesh):
    return jax.shard_map(
        per_device,
        mesh=mesh,
        in_specs=(
            P("dp", "seq", None),
            P("dp", "seq", None),
            P(),
            P(),
            P(),
            P(),
            P("seq", None, None, None),
            P("seq", None, None),
        ),
        out_specs=(
            P("dp", "seq", None),
            P("seq", None, None, None),
            P("seq", None, None),
            P(),
            P(),
            P(),
            P(),
        ),
        check_vma=False,
    )
```

profile of v0, /device:TPU:1, one launch (start us, length us, event | category | flops | bytes accessed | tf_op | source)
XLA Modules:
  0.0 787.0 jit_solution(7601056932142582993)
XLA Ops:
  8.8 2.3 convolution_bitcast_fusion.2
  11.2 7.8 collective-permute-start
  20.1 2.4 all_to_all.23
  22.5 6.5 all-to-all-start
  30.8 45.8 %all-to-all-done = f32[32,1,3072]{2,1,0:T(1,128)} async-done(((f32[32,1,3072]{2,1,0:T(1,128)}), f32[32,1,3072]{2,1,0:T(1,128)}, u32[]{:S(2)}, u32[]{:S(2)}) %all-to-all-start) | async-done | bytes 393248 | tf_op jit(solution)/shard_map/all_to_all | solution.py:45
  76.6 6.7 all-to-all-start.1
  83.9 2.4 collective-permute-done.1
  89.1 18.3 %all-to-all-done.1 = f32[32,64,128]{2,1,0:T(8,128)} async-done(((f32[32,64,128]{2,1,0:T(8,128)}), f32[32,64,128]{2,1,0:T(8,128)}, u32[]{:S(2)}, u32[]{:S(2)}) %all-to-all-start.1) | async-done | bytes 1048608 | tf_op jit(solution)/shard_map/all_to_all | solution.py:45
  107.4 10.3 %all-to-all-start.2 = ((f32[32,64,128]{2,1,0:T(8,128)}), f32[32,64,128]{2,1,0:T(8,128)S(1)}, u32[]{:S(2)}, u32[]{:S(2)}) async-start(f32[32,64,128]{2,1,0:T(8,128)} %bitcast.126), calls=%async_computation.2 | async-start | bytes 2097152 | tf_op jit(solution)/shard_map/all_to_all | solution.py:45
  123.8 4.5 convolution_bitcast_fusion
  128.3 13.4 %all-to-all-done.2 = f32[32,64,128]{2,1,0:T(8,128)S(1)} async-done(((f32[32,64,128]{2,1,0:T(8,128)}), f32[32,64,128]{2,1,0:T(8,128)S(1)}, u32[]{:S(2)}, u32[]{:S(2)}) %all-to-all-start.2) | async-done | bytes 1048608 | tf_op jit(solution)/shard_map/all_to_all | solution.py:45
  141.7 1.8 fusion.17
  143.6 4.0 add_multiply_fusion
  147.5 4.8 fusion.2
  152.4 3.2 convolution_bitcast_fusion.3
  155.5 1.6 reshape.135
  157.1 3.6 convolution_bitcast_fusion.4
  163.3 9.5 %all-to-all-start.4 = ((f32[32,1,3072]{2,1,0:T(1,128)}), f32[32,1,3072]{2,1,0:T(1,128)S(1)}, u32[]{:S(2)}, u32[]{:S(2)}) async-start(f32[32,1,3072]{2,1,0:T(1,128)} %copy.60), calls=%async_computation.4 | async-start | bytes 786432 | tf_op jit(solution)/shard_map/all_to_all | solution.py:45
  172.8 5.2 fusion.12
  178.1 6.2 convolution_add_fusion
  184.3 4.2 all-to-all-done.4
  189.2 5.6 all-to-all-start.3
  196.0 2.7 reduce
  198.7 2.0 reshape.136
  203.8 15.5 %all-to-all-done.3 = f32[32,64,128]{2,1,0:T(8,128)S(1)} async-done(((f32[32,64,128]{2,1,0:T(8,128)}), f32[32,64,128]{2,1,0:T(8,128)S(1)}, u32[]{:S(2)}, u32[]{:S(2)}) %all-to-all-start.3) | async-done | bytes 1048608 | tf_op jit(solution)/shard_map/all_to_all | solution.py:45
  223.1 55.9 %all-reduce.10.cloned.1.call-done = (f32[4,2,16,256]{3,1,0,2:T(2,128)}, f32[8,16,128]{2,0,1:T(8,128)}) async-done(((f32[4,2,16,256]{3,1,0,2:T(2,128)}, f32[8,16,128]{2,0,1:T(8,128)}), (f32[4,2,16,256]{3,1,0,2:T(2,128)}, f32[8,16,128]{2,0,1:T(8,128)})) %all-reduce.10.cloned.1.call-update) | async-done | bytes 196624 | tf_op jit(solution)/shard_map/psum | solution.py:111
  282.9 2.3 multiply_reduce_fusion.3
  287.1 4.6 collective-permute-start.3
  291.7 246.4 %all-reduce.8.cloned.1.call-done = (f32[2,2,2048]{2,1,0:T(2,128)}, f32[2,2,2048]{2,1,0:T(2,128)}, f32[2048]{0:T(1024)}) async-done(((f32[2,2,2048]{2,1,0:T(2,128)}, f32[2,2,2048]{2,1,0:T(2,128)}, f32[2048]{0:T(1024)}), (f32[2,2,2048]{2,1,0:T(2,128)}, f32[2,2,2048]{2,1,0:T(2,128)}, f32[2048]{0:T(1024)})) %all-reduce.8.cloned.1.call-update) | async-done | bytes 73744 | tf_op jit(solution)/shard_map/psum | solution.py:122
  542.2 2.9 fusion.6
  545.2 3.3 fusion.1
  548.5 229.4 %all-reduce.6.cloned.1.call-done = f32[128,128]{1,0:T(8,128)} async-done(((f32[128,128]{1,0:T(8,128)}), f32[128,128]{1,0:T(8,128)}) %all-reduce.6.cloned.1.call-update) | async-done | bytes 65552 | tf_op jit(solution)/shard_map/psum | solution.py:122
  (126 shorter events, 35.7 us)
Async XLA Ops:
  8.0 11.0 %copy-start.24 = (f32[8,16,128]{2,1,0:T(8,128)S(1)}, f32[8,16,128]{2,1,0:T(8,128)}, u32[]{:S(2)}) copy-start(f32[8,16,128]{2,1,0:T(8,128)} %param.15) | copy-start | bytes 196612
  8.0 11.0 %copy-start.15 = (f32[4,2,16,256]{3,2,1,0:T(8,128)S(1)}, f32[4,2,16,256]{3,2,1,0:T(8,128)}, u32[]{:S(2)}) copy-start(f32[4,2,16,256]{3,2,1,0:T(8,128)} %param.14) | copy-start | bytes 393220
  11.1 72.2 %copy-start.2 = (f32[128,2048]{1,0:T(8,128)}, f32[128,2048]{1,0:T(8,128)S(1)}, u32[]{:S(2)}) copy-start(f32[128,2048]{1,0:T(8,128)S(1)} %convolution_bitcast_fusion.2) | copy-start | bytes 3145732
  11.1 17.9 %copy-start.8 = (f32[1,128,2048]{2,1,0:T(8,128)S(1)}, f32[1,128,2048]{2,1,0:T(8,128)}, u32[]{:S(2)}) copy-start(f32[1,128,2048]{2,1,0:T(8,128)} %param.9) | copy-start | bytes 3145732
  11.2 72.1 %collective-permute-start = (f32[128,2048]{1,0:T(8,128)S(1)}, f32[128,2048]{1,0:T(8,128)S(1)}, u32[]{:S(2)}, u32[]{:S(2)}) collective-permute-start(f32[128,2048]{1,0:T(8,128)S(1)} %convolution_bitcast_fusion.2), channel_id=1, source_target_pairs={{0,16},{16,0},{1,17},{17,1},{2,18},{18,2},{3,19},{19,3},{4,20},{20... | collective-permute-start | bytes 3145736 | tf_op jit(solution)/shard_map/ppermute | solution.py:21
  22.5 54.1 %all-to-all-start = ((f32[32,1,3072]{2,1,0:T(1,128)}), f32[32,1,3072]{2,1,0:T(1,128)}, u32[]{:S(2)}, u32[]{:S(2)}) async-start(f32[32,1,3072]{2,1,0:T(1,128)} %all_to_all.23), calls=%async_computation | async-start | bytes 786432 | tf_op jit(solution)/shard_map/all_to_all | solution.py:45
  30.7 52.7 %copy-start.18 = (f32[1,1,2048]{2,1,0:T(1,128)}, f32[1,1,2048]{2,1,0:T(1,128)S(1)}, u32[]{:S(2)}) copy-start(f32[1,1,2048]{2,1,0:T(1,128)S(1)} %get-tuple-element.51) | copy-start | bytes 24580
  30.7 55.5 %copy-start.20 = (f32[1,1,2048]{2,1,0:T(1,128)}, f32[1,1,2048]{2,1,0:T(1,128)S(1)}, u32[]{:S(2)}) copy-start(f32[1,1,2048]{2,1,0:T(1,128)S(1)} %get-tuple-element.45) | copy-start | bytes 24580
  30.8 55.5 %copy-start.22 = (f32[1,1,2048]{2,1,0:T(1,128)}, f32[1,1,2048]{2,1,0:T(1,128)S(1)}, u32[]{:S(2)}) copy-start(f32[1,1,2048]{2,1,0:T(1,128)S(1)} %get-tuple-element.46) | copy-start | bytes 24580
  76.6 30.8 %all-to-all-start.1 = ((f32[32,64,128]{2,1,0:T(8,128)}), f32[32,64,128]{2,1,0:T(8,128)}, u32[]{:S(2)}, u32[]{:S(2)}) async-start(f32[32,64,128]{2,1,0:T(8,128)} %bitcast.14), calls=%async_computation.1 | async-start | bytes 2097152 | tf_op jit(solution)/shard_map/all_to_all | solution.py:45
  83.3 3.0 copy-start.1
  83.3 3.4 copy-start.5
  83.5 3.2 copy-start.3
  83.5 2.7 collective-permute-start.1
  107.4 34.3 %all-to-all-start.2 = ((f32[32,64,128]{2,1,0:T(8,128)}), f32[32,64,128]{2,1,0:T(8,128)S(1)}, u32[]{:S(2)}, u32[]{:S(2)}) async-start(f32[32,64,128]{2,1,0:T(8,128)} %bitcast.126), calls=%async_computation.2 | async-start | bytes 2097152 | tf_op jit(solution)/shard_map/all_to_all | solution.py:45
  123.8 17.9 %copy-start.13 = (f32[128,1,256]{2,1,0:T(1,128)S(1)}, f32[128,1,256]{2,1,0:T(1,128)}, u32[]{:S(2)}) copy-start(f32[128,1,256]{2,1,0:T(1,128)} %get-tuple-element.43) | copy-start | bytes 393220
  128.3 15.2 %copy-start.14 = (f32[128,1,256]{2,1,0:T(1,128)S(1)}, f32[128,1,256]{2,1,0:T(1,128)}, u32[]{:S(2)}) copy-start(f32[128,1,256]{2,1,0:T(1,128)} %get-tuple-element.44) | copy-start | bytes 393220
  147.5 4.9 copy-start.31
  157.1 3.6 copy-start.16
  163.3 25.2 %all-to-all-start.4 = ((f32[32,1,3072]{2,1,0:T(1,128)}), f32[32,1,3072]{2,1,0:T(1,128)S(1)}, u32[]{:S(2)}, u32[]{:S(2)}) async-start(f32[32,1,3072]{2,1,0:T(1,128)} %copy.60), calls=%async_computation.4 | async-start | bytes 786432 | tf_op jit(solution)/shard_map/all_to_all | solution.py:45
  172.8 5.3 copy-start.11
  189.2 30.1 %all-to-all-start.3 = ((f32[32,64,128]{2,1,0:T(8,128)}), f32[32,64,128]{2,1,0:T(8,128)S(1)}, u32[]{:S(2)}, u32[]{:S(2)}) async-start(f32[32,64,128]{2,1,0:T(8,128)} %bitcast.132), calls=%async_computation.3 | async-start | bytes 2097152 | tf_op jit(solution)/shard_map/all_to_all | solution.py:45
  194.9 84.2 %all-reduce.10.cloned.1.call-start = ((), (), s32[]{:S(2)}) async-start(), calls=%async_computation.7 | async-start | bytes 393216 | tf_op jit(solution)/shard_map/psum | solution.py:111
  202.9 17.1 %copy-start.28 = (f32[128]{0:T(128)S(1)}, f32[128]{0:T(128)}, u32[]{:S(2)}) copy-start(f32[128]{0:T(128)} %copy-done.27) | copy-start | bytes 1540
  203.5 334.6 %all-reduce.8.cloned.1.call-start = ((), (), s32[]{:S(2)}) async-start(), calls=%async_computation.6 | async-start | bytes 147456 | tf_op jit(solution)/shard_map/psum | solution.py:122
  222.2 60.1 %copy-start.30 = (f32[2]{0:T(128)S(1)}, f32[2]{0:T(128)}, u32[]{:S(2)}) copy-start(f32[2]{0:T(128)} %compare_convert_fusion) | copy-start | bytes 28
  222.2 60.8 %copy-start.21 = (f32[1,1,2048]{2,1,0:T(1,128)S(1)}, f32[1,1,2048]{2,1,0:T(1,128)}, u32[]{:S(2)}) copy-start(f32[1,1,2048]{2,1,0:T(1,128)} %copy-done.20) | copy-start | bytes 24580
  222.3 60.6 %collective-permute-start.2 = (f32[128,2048]{1,0:T(8,128)S(1)}, f32[128,2048]{1,0:T(8,128)}, u32[]{:S(2)}, u32[]{:S(2)}) collective-permute-start(f32[128,2048]{1,0:T(8,128)S(1)} %broadcast_multiply_fusion), channel_id=1, source_target_pairs={{0,1},{1,0},{2,3},{3,2},{4,5},{5,4},{6,7},{7,6},{8,9},{9,8},{10,11... | collective-permute-start | bytes 3145736 | tf_op jit(solution)/shard_map/ppermute | solution.py:21
  282.9 2.3 copy-start.29
  282.9 3.1 copy-start.19
  286.0 491.9 %all-reduce.6.cloned.1.call-start = ((), (), s32[]{:S(2)}) async-start(), calls=%async_computation.5 | async-start | bytes 131072 | tf_op jit(solution)/shard_map/psum | solution.py:122
  287.1 255.1 %collective-permute-start.3 = (f32[128,2048]{1,0:T(8,128)}, f32[128,2048]{1,0:T(8,128)}, u32[]{:S(2)}, u32[]{:S(2)}) collective-permute-start(f32[128,2048]{1,0:T(8,128)} %broadcast_multiply_fusion.1), channel_id=1, source_target_pairs={{0,16},{16,0},{1,17},{17,1},{2,18},{18,2},{3,19},{19,3},{4,20},{20... | collective-permute-start | bytes 3145736 | tf_op jit(solution)/shard_map/ppermute | solution.py:21
  (12 other events, 15.5 us)
Sparse Core Ops, SparseCore 0:
  203.7 75.3 all-reduce.9
Sparse Core Ops, SparseCore 1:
  286.0 252.0 all-reduce.7
  545.2 232.6 all-reduce.5
where the time goes:
time: 794 us; the launch traced here: 787 us
  waiting for transfers between devices  631 us (79%)
  starting transfers between devices  52.6 us (7%)
  matrix products  41.9 us (5%)
  local copies, waits for them, and re-layouts  23.6 us (3%)
  other arithmetic  21.3 us (3%)
  between operations  16.3 us (2%)
    psum x2, waiting for transfers between devices, per_device(): lax.psum((term_block, term_hi, term_lo, grad_gain_local), ('dp', 'seq'))  476 us
    all_to_all x5, waiting for transfers between devices, exchange(): return lax.all_to_all(x, 'seq', 0, 0, tiled=True)  97.2 us
    psum x1, waiting for transfers between devices, per_device(): part_gu, part_down = lax.psum((part_gu, part_down), 'dp')  55.9 us
    all_to_all x5, starting transfers between devices, exchange(): return lax.all_to_all(x, 'seq', 0, 0, tiled=True)  38.6 us
  transfers between devices with their start and end apart: 12, of which 9 were waited for; matrix products, arithmetic and copies ran while one was open for 6% of the time, Pallas kernels for 0%

commit v1 on v0

--- a/solution.py
+++ b/solution.py
@@ -3,6 +3,7 @@
 import jax.numpy as jnp
 from jax import lax
 from jax.sharding import PartitionSpec as P
+from jax.lax import psum
 
 NB = 16
 BLK = 128
@@ -61,6 +62,11 @@
 
 
 def per_device(inputs, cotangent, block_mix, twist_hi, twist_lo, gain, gate_up, down):
+
+    def attach_the_vector(dev_axis, peer_axis, panel):
+        local_part = psum(psum(panel, peer_axis), dev_axis)
+        return local_part
+
     seq_in = inputs[0]
     tokens, width = seq_in.shape
     count = lax.axis_size("seq")
@@ -119,8 +125,8 @@
     term_block = jnp.einsum("kid,kjd->ij", grad_mb, xb, precision=HIGH)
     grad_seq = jnp.einsum("ij,kid->kjd", block_mix, grad_mb, precision=HIGH).reshape(tokens, width)
     grad_seq = grad_seq + grad_resid
-    sum_block, sum_hi, sum_lo, sum_gain = lax.psum(
-        (term_block, term_hi, term_lo, grad_gain_local), ("dp", "seq")
+    sum_block, sum_hi, sum_lo, sum_gain = attach_the_vector(
+        "dp", "seq", (term_block, term_hi, term_lo, grad_gain_local)
     )
     factor = 1.0 / math.sqrt(lax.axis_size("dp") * count * tokens)
     return (

time: 794 us -> 917 us (1.15)
  waiting for transfers between devices: 631 us -> 750 us
    psum x2 -> x3, waiting for transfers between devices: 476 us -> 581 us  [attach_the_vector(): local_part = psum(psum(panel, peer_axis), dev_axis)]
    psum x1, waiting for transfers between devices: 55.9 us -> 71.6 us  [per_device(): part_gu, part_down = lax.psum((part_gu, part_down), 'dp')]
  transfers between devices with their start and end apart: 12 -> 13, of which waited for: 9 -> 10; matrix products, arithmetic and copies ran while one was open for 6% -> 6% of each run, Pallas kernels for 0% -> 0%
where the time goes in v1:
time: 917 us; the launch traced here: 906 us
  waiting for transfers between devices  750 us (82%)
  starting transfers between devices  57.5 us (6%)
  matrix products  38.1 us (4%)
  local copies, waits for them, and re-layouts  27.2 us (3%)
  other arithmetic  18.8 us (2%)
  between operations  14.5 us (2%)
    psum x3, waiting for transfers between devices, attach_the_vector(): local_part = psum(psum(panel, peer_axis), dev_axis)  581 us
    all_to_all x5, waiting for transfers between devices, exchange(): return lax.all_to_all(x, 'seq', 0, 0, tiled=True)  95.1 us
    psum x1, waiting for transfers between devices, per_device(): part_gu, part_down = lax.psum((part_gu, part_down), 'dp')  71.6 us
    all_to_all x5, starting transfers between devices, exchange(): return lax.all_to_all(x, 'seq', 0, 0, tiled=True)  42.8 us
  transfers between devices with their start and end apart: 13, of which 10 were waited for; matrix products, arithmetic and copies ran while one was open for 6% of the time, Pallas kernels for 0%

profile of v1, /device:TPU:1, one launch (start us, length us, event | category | flops | bytes accessed | tf_op | source)
XLA Modules:
  0.0 905.9 jit_solution(9122463818548406592)
XLA Ops:
  8.0 2.3 convolution_bitcast_fusion.2
  10.3 7.8 collective-permute-start
  19.3 2.4 all_to_all.23
  21.7 6.5 all-to-all-start
  29.9 45.8 %all-to-all-done = f32[32,1,3072]{2,1,0:T(1,128)} async-done(((f32[32,1,3072]{2,1,0:T(1,128)}), f32[32,1,3072]{2,1,0:T(1,128)}, u32[]{:S(2)}, u32[]{:S(2)}) %all-to-all-start) | async-done | bytes 393248 | tf_op jit(solution)/shard_map/all_to_all | solution.py:46
  75.8 6.7 all-to-all-start.1
  83.0 2.4 collective-permute-done.1
  88.0 18.5 %all-to-all-done.1 = f32[32,64,128]{2,1,0:T(8,128)} async-done(((f32[32,64,128]{2,1,0:T(8,128)}), f32[32,64,128]{2,1,0:T(8,128)}, u32[]{:S(2)}, u32[]{:S(2)}) %all-to-all-start.1) | async-done | bytes 1048608 | tf_op jit(solution)/shard_map/all_to_all | solution.py:46
  106.5 10.3 %all-to-all-start.2 = ((f32[32,64,128]{2,1,0:T(8,128)}), f32[32,64,128]{2,1,0:T(8,128)S(1)}, u32[]{:S(2)}, u32[]{:S(2)}) async-start(f32[32,64,128]{2,1,0:T(8,128)} %bitcast.125), calls=%async_computation.2 | async-start | bytes 2097152 | tf_op jit(solution)/shard_map/all_to_all | solution.py:46
  123.0 4.5 convolution_bitcast_fusion
  127.5 13.4 %all-to-all-done.2 = f32[32,64,128]{2,1,0:T(8,128)S(1)} async-done(((f32[32,64,128]{2,1,0:T(8,128)}), f32[32,64,128]{2,1,0:T(8,128)S(1)}, u32[]{:S(2)}, u32[]{:S(2)}) %all-to-all-start.2) | async-done | bytes 1048608 | tf_op jit(solution)/shard_map/all_to_all | solution.py:46
  142.7 2.6 add_multiply_fusion
  145.3 3.6 fusion.12
  149.0 4.8 convolution_add_fusion
  153.7 9.5 %all-to-all-start.3 = ((f32[32,64,128]{2,1,0:T(8,128)}), f32[32,64,128]{2,1,0:T(8,128)}, u32[]{:S(2)}, u32[]{:S(2)}) async-start(f32[32,64,128]{2,1,0:T(8,128)} %bitcast.131), calls=%async_computation.3 | async-start | bytes 2097152 | tf_op jit(solution)/shard_map/all_to_all | solution.py:46
  163.3 4.2 convolution_bitcast_fusion.4
  167.5 4.9 fusion.2
  172.4 3.2 convolution_bitcast_fusion.3
  175.6 11.8 %all-to-all-done.3 = f32[32,64,128]{2,1,0:T(8,128)} async-done(((f32[32,64,128]{2,1,0:T(8,128)}), f32[32,64,128]{2,1,0:T(8,128)}, u32[]{:S(2)}, u32[]{:S(2)}) %all-to-all-start.3) | async-done | bytes 1048608 | tf_op jit(solution)/shard_map/all_to_all | solution.py:46
  187.4 2.0 copy.56
  198.5 9.8 %all-to-all-start.4 = ((f32[32,1,3072]{2,1,0:T(1,128)}), f32[32,1,3072]{2,1,0:T(1,128)}, u32[]{:S(2)}, u32[]{:S(2)}) async-start(f32[32,1,3072]{2,1,0:T(1,128)} %copy.60), calls=%async_computation.4 | async-start | bytes 786432 | tf_op jit(solution)/shard_map/all_to_all | solution.py:46
  209.0 2.2 multiply_reduce_fusion.3
  212.3 5.3 collective-permute-start.3
  218.4 5.6 all-to-all-done.4
  224.0 2.7 reduce
  226.7 2.0 reshape.136
  230.1 260.0 %all-reduce.10.cloned.1.call-done = (f32[2,2,2048]{2,1,0:T(2,128)}, f32[2,2,2048]{2,1,0:T(2,128)}, f32[2048]{0:T(1024)}) async-done(((f32[2,2,2048]{2,1,0:T(2,128)}, f32[2,2,2048]{2,1,0:T(2,128)}, f32[2048]{0:T(1024)}), (f32[2,2,2048]{2,1,0:T(2,128)}, f32[2,2,2048]{2,1,0:T(2,128)}, f32[2048]{0:T(1024)})) %all-reduce.10.cloned.1.call-update) | async-done | bytes 73744 | tf_op jit(solution)/shard_map/psum | solution.py:67
  493.1 66.9 %all-reduce.12.cloned.1.call-done = (f32[2,2,2048]{2,1,0:T(2,128)}, f32[2,2,2048]{2,1,0:T(2,128)}, f32[2048]{0:T(1024)}) async-done(((f32[2,2,2048]{2,1,0:T(2,128)}, f32[2,2,2048]{2,1,0:T(2,128)}, f32[2048]{0:T(1024)}), (f32[2,2,2048]{2,1,0:T(2,128)}, f32[2,2,2048]{2,1,0:T(2,128)}, f32[2048]{0:T(1024)})) %all-reduce.12.cloned.1.call-update) | async-done | bytes 73744 | tf_op jit(solution)/shard_map/psum | solution.py:67
  561.4 2.9 fusion.6
  565.0 253.9 %all-reduce.8.cloned.1.call-done = f32[128,128]{1,0:T(8,128)} async-done(((f32[128,128]{1,0:T(8,128)}), f32[128,128]{1,0:T(8,128)}) %all-reduce.8.cloned.1.call-update) | async-done | bytes 65552 | tf_op jit(solution)/shard_map/psum | solution.py:67
  819.6 3.3 fusion.1
  822.9 71.6 %all-reduce.14.cloned.1.call-done = (f32[4,2,16,256]{3,1,0,2:T(2,128)}, f32[8,16,128]{2,0,1:T(8,128)}, f32[128,128]{1,0:T(8,128)}) async-done(((f32[4,2,16,256]{3,1,0,2:T(2,128)}, f32[8,16,128]{2,0,1:T(8,128)}, f32[128,128]{1,0:T(8,128)}), (f32[4,2,16,256]{3,1,0,2:T(2,128)}, f32[8,16,128]{2,0,1:T(8,128)}, f32[128,128]{1,0:T(8,128)})) %all-reduce.14.cloned.1.call-update) | async-done | bytes 262160 | tf_op jit(solution)/shard_map/psum | solution.py:117
  (121 shorter events, 38.1 us)
Async XLA Ops:
  7.2 11.0 %copy-start.21 = (f32[8,16,128]{2,1,0:T(8,128)S(1)}, f32[8,16,128]{2,1,0:T(8,128)}, u32[]{:S(2)}) copy-start(f32[8,16,128]{2,1,0:T(8,128)} %param.15) | copy-start | bytes 196612
  7.2 11.0 %copy-start.18 = (f32[4,2,16,256]{3,2,1,0:T(8,128)S(1)}, f32[4,2,16,256]{3,2,1,0:T(8,128)}, u32[]{:S(2)}) copy-start(f32[4,2,16,256]{3,2,1,0:T(8,128)} %param.14) | copy-start | bytes 393220
  10.3 72.2 %copy-start.2 = (f32[128,2048]{1,0:T(8,128)}, f32[128,2048]{1,0:T(8,128)S(1)}, u32[]{:S(2)}) copy-start(f32[128,2048]{1,0:T(8,128)S(1)} %convolution_bitcast_fusion.2) | copy-start | bytes 3145732
  10.3 17.9 %copy-start.9 = (f32[1,128,2048]{2,1,0:T(8,128)S(1)}, f32[1,128,2048]{2,1,0:T(8,128)}, u32[]{:S(2)}) copy-start(f32[1,128,2048]{2,1,0:T(8,128)} %param.9) | copy-start | bytes 3145732
  10.3 72.1 %collective-permute-start = (f32[128,2048]{1,0:T(8,128)S(1)}, f32[128,2048]{1,0:T(8,128)S(1)}, u32[]{:S(2)}, u32[]{:S(2)}) collective-permute-start(f32[128,2048]{1,0:T(8,128)S(1)} %convolution_bitcast_fusion.2), channel_id=1, source_target_pairs={{0,16},{16,0},{1,17},{17,1},{2,18},{18,2},{3,19},{19,3},{4,20},{20... | collective-permute-start | bytes 3145736 | tf_op jit(solution)/shard_map/ppermute | solution.py:22
  21.7 54.1 %all-to-all-start = ((f32[32,1,3072]{2,1,0:T(1,128)}), f32[32,1,3072]{2,1,0:T(1,128)}, u32[]{:S(2)}, u32[]{:S(2)}) async-start(f32[32,1,3072]{2,1,0:T(1,128)} %all_to_all.23), calls=%async_computation | async-start | bytes 786432 | tf_op jit(solution)/shard_map/all_to_all | solution.py:46
  75.8 30.8 %all-to-all-start.1 = ((f32[32,64,128]{2,1,0:T(8,128)}), f32[32,64,128]{2,1,0:T(8,128)}, u32[]{:S(2)}, u32[]{:S(2)}) async-start(f32[32,64,128]{2,1,0:T(8,128)} %bitcast.14), calls=%async_computation.1 | async-start | bytes 2097152 | tf_op jit(solution)/shard_map/all_to_all | solution.py:46
  82.4 3.0 copy-start.1
  82.5 2.9 copy-start.6
  82.6 3.2 copy-start.3
  82.7 2.7 collective-permute-start.1
  106.5 34.3 %all-to-all-start.2 = ((f32[32,64,128]{2,1,0:T(8,128)}), f32[32,64,128]{2,1,0:T(8,128)S(1)}, u32[]{:S(2)}, u32[]{:S(2)}) async-start(f32[32,64,128]{2,1,0:T(8,128)} %bitcast.125), calls=%async_computation.2 | async-start | bytes 2097152 | tf_op jit(solution)/shard_map/all_to_all | solution.py:46
  123.0 17.9 %copy-start.16 = (f32[128,1,256]{2,1,0:T(1,128)S(1)}, f32[128,1,256]{2,1,0:T(1,128)}, u32[]{:S(2)}) copy-start(f32[128,1,256]{2,1,0:T(1,128)} %get-tuple-element.47) | copy-start | bytes 393220
  127.5 15.2 %copy-start.17 = (f32[128,1,256]{2,1,0:T(1,128)S(1)}, f32[128,1,256]{2,1,0:T(1,128)}, u32[]{:S(2)}) copy-start(f32[128,1,256]{2,1,0:T(1,128)} %get-tuple-element.48) | copy-start | bytes 393220
  145.3 8.4 copy-start.5
  145.3 8.4 copy-start.26
  153.7 33.7 %all-to-all-start.3 = ((f32[32,64,128]{2,1,0:T(8,128)}), f32[32,64,128]{2,1,0:T(8,128)}, u32[]{:S(2)}, u32[]{:S(2)}) async-start(f32[32,64,128]{2,1,0:T(8,128)} %bitcast.131), calls=%async_computation.3 | async-start | bytes 2097152 | tf_op jit(solution)/shard_map/all_to_all | solution.py:46
  163.3 4.2 copy-start.14
  167.5 4.9 copy-start.12
  167.5 4.9 copy-start.27
  187.4 3.3 copy-start.4
  187.4 3.3 copy-start.8
  187.4 3.3 copy-start.10
  191.7 17.3 %collective-permute-start.2 = (f32[128,2048]{1,0:T(8,128)S(1)}, f32[128,2048]{1,0:T(8,128)}, u32[]{:S(2)}, u32[]{:S(2)}) collective-permute-start(f32[128,2048]{1,0:T(8,128)S(1)} %broadcast_multiply_fusion), channel_id=1, source_target_pairs={{0,1},{1,0},{2,3},{3,2},{4,5},{5,4},{6,7},{7,6},{8,9},{9,8},{10,11... | collective-permute-start | bytes 3145736 | tf_op jit(solution)/shard_map/ppermute | solution.py:22
  198.5 25.5 %all-to-all-start.4 = ((f32[32,1,3072]{2,1,0:T(1,128)}), f32[32,1,3072]{2,1,0:T(1,128)}, u32[]{:S(2)}, u32[]{:S(2)}) async-start(f32[32,1,3072]{2,1,0:T(1,128)} %copy.60), calls=%async_computation.4 | async-start | bytes 786432 | tf_op jit(solution)/shard_map/all_to_all | solution.py:46
  208.3 281.9 %all-reduce.10.cloned.1.call-start = ((), (), s32[]{:S(2)}) async-start(), calls=%async_computation.6 | async-start | bytes 147456 | tf_op jit(solution)/shard_map/psum | solution.py:67
  212.3 349.1 %collective-permute-start.3 = (f32[128,2048]{1,0:T(8,128)}, f32[128,2048]{1,0:T(8,128)}, u32[]{:S(2)}, u32[]{:S(2)}) collective-permute-start(f32[128,2048]{1,0:T(8,128)} %broadcast_multiply_fusion.1), channel_id=1, source_target_pairs={{0,16},{16,0},{1,17},{17,1},{2,18},{18,2},{3,19},{19,3},{4,20},{20... | collective-permute-start | bytes 3145736 | tf_op jit(solution)/shard_map/ppermute | solution.py:22
  218.4 341.6 %all-reduce.12.cloned.1.call-start = ((), (), s32[]{:S(2)}) async-start(), calls=%async_computation.7 | async-start | bytes 147456 | tf_op jit(solution)/shard_map/psum | solution.py:67
  490.2 328.7 %all-reduce.8.cloned.1.call-start = ((), (), s32[]{:S(2)}) async-start(), calls=%async_computation.5 | async-start | bytes 131072 | tf_op jit(solution)/shard_map/psum | solution.py:67
  560.0 4.4 copy-start.22
  560.0 258.9 %copy-start.23 = (f32[2048]{0:T(1024)S(1)}, f32[2048]{0:T(1024)}, u32[]{:S(2)}) copy-start(f32[2048]{0:T(1024)} %get-tuple-element.39) | copy-start | bytes 24580
  564.4 330.2 %all-reduce.14.cloned.1.call-start = ((), (), s32[]{:S(2)}) async-start(), calls=%async_computation.8 | async-start | bytes 524288 | tf_op jit(solution)/shard_map/psum | solution.py:117
  (9 other events, 12.3 us)
Sparse Core Ops, SparseCore 0:
  218.5 271.6 all-reduce.9
  493.2 66.7 all-reduce.11
  564.5 254.4 all-reduce.7
  822.4 72.1 all-reduce.13
